TPU v7x, 256 devices: a whole 4x4x8 slice. The times are simulated.
256 devices in a mesh: seq: 64 (over y, z, core), ch: 4 (over x).
Axes of the slice: x: 4, y: 4, z: 8, core: 2. Of those that a mesh axis runs over, the one named last changes fastest.
Arguments:
- query_stream: bfloat16 [16384, 4096], P('seq', 'ch'), may hold values from -16 to 16
- key_stream: bfloat16 [16384, 4096], P('seq', 'ch'), may hold values from -6 to 6
- value_stream: bfloat16 [16384, 4096], P('seq', 'ch'), may hold values from -6 to 6
- filter_taps: float32 [4096, 128], P('ch'), may hold values from -0.5 to 0.5
- out_weight: bfloat16 [4096, 4096], P('seq', 'ch'), may hold values from -0.09375 to 0.09375
- upstream: bfloat16 [16384, 4096], P('seq', 'ch'), may hold values from -6 to 6
Outputs:
- mixed: bfloat16 [16384, 4096], P('seq', 'ch')
- grad_query: bfloat16 [16384, 4096], P('seq', 'ch')
- grad_key: bfloat16 [16384, 4096], P('seq', 'ch')
- grad_value: bfloat16 [16384, 4096], P('seq', 'ch')
- grad_filter: float32 [4096, 128], P('ch')
- grad_weight: float32 [4096, 4096], P('seq', 'ch')
All inputs are finite; a program needn't handle non-finite values.
Results may differ from a plain program's by a relative error of at most 0.0057.
Values may be sent and summed in bfloat16 or wider, within the bound.
No kernel may reach another device: no remote copies, remote signals or barrier semaphores. Data moves between devices by JAX's collectives and lax.ppermute only.
A program may use at most 128 MiB of HBM per device.

v0:
```python
import jax
import jax.numpy as jnp
from jax import lax
from jax.sharding import PartitionSpec as P


def from_behind(value, axis, steps):
    count = lax.axis_size(axis)
    initial, last = (max(0, -steps), min(count, count - steps))
    return lax.ppermute(value, axis, [(source, source + steps) for source in range(initial, last)])


def depthwise(signal, kernel):
    output = lax.conv_general_dilated(
        signal[None],
        kernel[:, None, :],
        (1,),
        "VALID",
        dimension_numbers=("NWC", "WIO", "NWC"),
        feature_group_count=signal.shape[1],
        precision=lax.Precision.HIGHEST,
    )
    return output[0]


def body(query_stream, key_stream, value_stream, filter_taps, out_weight, upstream):
    rows_here = query_stream.shape[0]
    tap_count = filter_taps.shape[1]
    keyed = (key_stream.astype(jnp.float32) * value_stream.astype(jnp.float32)).astype(jnp.bfloat16)
    rim_before = from_behind(keyed[rows_here - (tap_count - 1) :], "seq", 1)
    front_pad = jnp.concatenate([rim_before, keyed], axis=0).astype(jnp.float32)
    response = depthwise(front_pad, filter_taps.T[::-1])
    query_wide = query_stream.astype(jnp.float32)
    gated = (query_wide * response).astype(jnp.bfloat16)
    gated_full = lax.all_gather(gated, "ch", axis=1, tiled=True)
    weight_cols = lax.all_gather(out_weight, "seq", axis=0, tiled=True)
    mixed = jnp.dot(gated_full, weight_cols, preferred_element_type=jnp.float32).astype(
        jnp.bfloat16
    )
    partial_terms = lax.dot_general(
        upstream, weight_cols, (((1,), (1,)), ((), ())), preferred_element_type=jnp.float32
    )
    grad_gated = lax.psum_scatter(partial_terms, "ch", scatter_dimension=1, tiled=True)
    grad_query = (grad_gated * response).astype(jnp.bfloat16)
    grad_response = grad_gated * query_wide
    rim_after = from_behind(grad_response[: tap_count - 1], "seq", -1)
    back_pad = jnp.concatenate([grad_response, rim_after], axis=0)
    grad_keyed = depthwise(back_pad, filter_taps.T)
    grad_key = (grad_keyed * value_stream.astype(jnp.float32)).astype(jnp.bfloat16)
    grad_value = (grad_keyed * key_stream.astype(jnp.float32)).astype(jnp.bfloat16)
    filter_local = depthwise(front_pad, grad_response)[::-1].T
    grad_filter = lax.psum(filter_local, "seq")
    columns = lax.slice_in_dim(gated_full, 0, lax.axis_size("seq") * out_weight.shape[0], axis=1)
    grad_weight = lax.psum_scatter(
        lax.dot_general(
            columns, upstream, (((0,), (0,)), ((), ())), preferred_element_type=jnp.float32
        ),
        "seq",
        scatter_dimension=0,
        tiled=True,
    )
    return (mixed, grad_query, grad_key, grad_value, grad_filter, grad_weight)


def solution(mesh):
    in_specs = (
        P("seq", "ch"),
        P("seq", "ch"),
        P("seq", "ch"),
        P("ch", None),
        P("seq", "ch"),
        P("seq", "ch"),
    )
    out_specs = (
        P("seq", "ch"),
        P("seq", "ch"),
        P("seq", "ch"),
        P("seq", "ch"),
        P("ch", None),
        P("seq", "ch"),
    )
    return jax.shard_map(body, mesh=mesh, in_specs=in_specs, out_specs=out_specs, check_vma=False)
```

profile of v0, /device:TPU:2, one launch (start us, length us, event | category | flops | bytes accessed | tf_op | source)
XLA Modules:
  0.0 614.4 jit_solution(9339220841736007042)
XLA Ops:
  7.2 0.0 copy-start
  7.2 0.0 all-gather.5.cloned.1.call-start
  7.2 0.7 all-gather.5.cloned.1.call-update
  7.9 0.0 reduce-scatter.3.cloned.1.call-start
  8.0 88.8 %all-gather.5.cloned.1.call-done = bf16[4096,1024]{1,0:T(8,128)(2,1)} async-done(((bf16[64,1024]{1,0:T(8,128)(2,1)}), bf16[4096,1024]{1,0:T(8,128)(2,1)}) %all-gather.5.cloned.1.call-update) | async-done | bytes 8388624 | tf_op jit(solution)/shard_map/all_gather | solution.py:36
  96.8 0.0 copy-done
  96.8 7.7 %fusion.12 = f32[256,4096]{1,0:T(8,128)} fusion(bf16[256,1024]{1,0:T(8,128)(2,1)S(1)} %copy-done, bf16[4096,1024]{1,0:T(8,128)(2,1)} %all-gather.5.cloned.1.call-done), kind=kOutput, calls=%fused_computation.22 | convolution fusion | flops 2147483648 | bytes 13107200 | tf_op jit(solution)/shard_map/dot_general | solution.py:40
  104.5 0.0 reduce-scatter.3.cloned.1.call-update
  104.5 0.0 copy-start.7
  104.5 0.0 all-gather.3.cloned.1.call-start
  104.5 45.0 %reduce-scatter.3.cloned.1.call-done = f32[256,1024]{1,0:T(8,128)} async-done(((f32[256,4096]{1,0:T(8,128)}), f32[256,1024]{1,0:T(8,128)}) %reduce-scatter.3.cloned.1.call-update) | async-done | bytes 1048592 | tf_op jit(solution)/shard_map/reduce_scatter | solution.py:43
  149.5 1.4 convert_multiply_fusion.3
  150.9 0.0 copy-start.1
  151.0 1.3 collective-permute-start.1
  152.3 0.4 copy.20
  152.7 2.2 collective-permute-done.1
  154.9 1.2 maximum_bitcast_fusion
  156.1 0.0 copy-start.9
  156.1 0.0 copy-start.10
  156.1 10.6 %fusion = f32[1,256,1024]{2,0,1:T(1,128)S(1)} fusion(f32[128,1,1024]{2,1,0:T(1,128)S(1)} %copy.20, f32[1,383,1024]{2,1,0:T(8,128)S(1)} %maximum_bitcast_fusion), kind=kOutput, calls=%fused_computation.1 | convolution fusion | flops 402653184 | bytes 3141632 | tf_op jit(solution)/shard_map/conv_general_dilated | solution.py:14
  166.7 0.0 copy-done.9
  166.7 0.0 copy-done.10
  166.7 0.0 copy-start.8
  166.7 1.5 fusion.7
  168.2 0.1 slice.8
  168.3 8.5 %collective-permute-start = (bf16[127,1024]{1,0:T(8,128)(2,1)S(1)}, bf16[127,1024]{1,0:T(8,128)(2,1)S(1)}, u32[]{:S(2)}, u32[]{:S(2)}) collective-permute-start(bf16[127,1024]{1,0:T(8,128)(2,1)S(1)} %slice.8), channel_id=1, source_target_pairs={{0,4},{4,8},{8,12},{12,16},{16,20},{20,24},{24,28},{28,32},{32,36}... | collective-permute-start | bytes 780296 | tf_op jit(solution)/shard_map/ppermute | solution.py:10
  176.8 0.7 rev.6
  177.6 0.4 copy.18
  178.0 0.0 collective-permute-done
  178.0 0.1 maximum_bitcast_fusion.1
  178.1 0.0 copy-start.3
  178.1 0.0 copy-start.6
  178.2 10.6 %fusion.4 = f32[1,256,1024]{2,0,1:T(1,128)S(1)} fusion(f32[128,1,1024]{2,1,0:T(1,128)S(1)} %copy.18, bf16[1,383,1024]{2,1,0:T(8,128)(2,1)S(1)} %maximum_bitcast_fusion.1), kind=kOutput, calls=%fused_computation.11 | convolution fusion | flops 402653184 | bytes 2357248 | tf_op jit(solution)/shard_map/conv_general_dilated | solution.py:14
  188.8 1.4 fusion.10
  190.2 0.0 all-gather.3.cloned.1.call-update
  190.2 0.0 all-reduce.2.cloned.1.call-start
  190.3 10.7 %fusion.2 = f32[1,128,1024]{2,0,1:T(1,128)S(1)} fusion(bf16[1,383,1024]{2,1,0:T(8,128)(2,1)S(1)} %maximum_bitcast_fusion.1, f32[256,1,1024]{2,0,1:T(8,128)S(1)} %bitcast.29), kind=kOutput, calls=%fused_computation.9 | convolution fusion | flops 402653184 | bytes 2357248 | tf_op jit(solution)/shard_map/conv_general_dilated | solution.py:14
  201.0 0.1 copy.40
  201.1 2.6 rev.7
  203.7 0.0 all-reduce.2.cloned.1.call-update
  203.7 0.2 reduce-scatter.5.cloned.1.call-start
  203.9 23.9 %all-gather.3.cloned.1.call-done = bf16[256,4096]{1,0:T(8,128)(2,1)} async-done(((bf16[256,1024]{1,0:T(8,128)(2,1)}), bf16[256,4096]{1,0:T(8,128)(2,1)}) %all-gather.3.cloned.1.call-update) | async-done | bytes 2097168 | tf_op jit(solution)/shard_map/all_gather | solution.py:35
  227.9 9.7 %fusion.13 = f32[4096,1024]{1,0:T(8,128)} fusion(bf16[256,4096]{1,0:T(8,128)(2,1)} %all-gather.3.cloned.1.call-done, bf16[256,1024]{1,0:T(8,128)(2,1)S(1)} %copy-done), kind=kOutput, calls=%fused_computation.23 | convolution fusion | flops 2147483648 | bytes 19398656 | tf_op jit(solution)/shard_map/dot_general | solution.py:55
  237.6 0.0 reduce-scatter.5.cloned.1.call-update
  237.6 178.5 %all-reduce.2.cloned.1.call-done = f32[1024,128]{0,1:T(8,128)} async-done(((f32[1024,128]{0,1:T(8,128)}), f32[1024,128]{0,1:T(8,128)}) %all-reduce.2.cloned.1.call-update) | async-done | bytes 524304 | tf_op jit(solution)/shard_map/psum | solution.py:52
  416.1 2.0 copy.23
  418.1 6.5 %convolution_convert_fusion = bf16[256,1024]{1,0:T(8,128)(2,1)} fusion(bf16[256,4096]{1,0:T(8,128)(2,1)S(1)} %copy-done.4, bf16[4096,1024]{1,0:T(8,128)(2,1)} %all-gather.5.cloned.1.call-done), kind=kOutput, calls=%fused_computation.8 | convolution fusion | flops 2147745792 | bytes 11010048 | tf_op jit(solution)/shard_map/dot_general | solution.py:37
  424.6 183.2 %reduce-scatter.5.cloned.1.call-done = f32[64,1024]{1,0:T(8,128)} async-done(((f32[4096,1024]{1,0:T(8,128)}), f32[64,1024]{1,0:T(8,128)}) %reduce-scatter.5.cloned.1.call-update) | async-done | bytes 262160 | tf_op jit(solution)/shard_map/reduce_scatter | solution.py:54
  (12 shorter events, 0.1 us)
Async XLA Ops:
  7.2 89.6 %copy-start = (bf16[256,1024]{1,0:T(8,128)(2,1)S(1)}, bf16[256,1024]{1,0:T(8,128)(2,1)}, u32[]{:S(2)}) copy-start(bf16[256,1024]{1,0:T(8,128)(2,1)} %param.11) | copy-start | bytes 1572868
  7.2 89.6 %all-gather.5.cloned.1.call-start = ((), (), s32[]{:S(2)}) async-start(), calls=%async_computation.3 | async-start | bytes 8519680 | tf_op jit(solution)/shard_map/all_gather | solution.py:36
  7.9 141.6 %reduce-scatter.3.cloned.1.call-start = ((), (), s32[]{:S(2)}) async-start(), calls=%async_computation.4 | async-start | bytes 5242880 | tf_op jit(solution)/shard_map/reduce_scatter | solution.py:43
  104.4 45.1 %copy-start.5 = (bf16[256,1024]{1,0:T(8,128)(2,1)S(1)}, bf16[256,1024]{1,0:T(8,128)(2,1)}, u32[]{:S(2)}) copy-start(bf16[256,1024]{1,0:T(8,128)(2,1)} %param.6) | copy-start | bytes 1572868
  104.5 47.8 %copy-start.7 = (f32[1024,128]{1,0:T(8,128)S(1)}, f32[1024,128]{1,0:T(8,128)}, u32[]{:S(2)}) copy-start(f32[1024,128]{1,0:T(8,128)} %param.9) | copy-start | bytes 1572868
  104.5 123.4 %all-gather.3.cloned.1.call-start = ((), (), s32[]{:S(2)}) async-start(), calls=%async_computation.2 | async-start | bytes 2621440 | tf_op jit(solution)/shard_map/all_gather | solution.py:35
  150.9 5.2 copy-start.1
  151.0 3.9 collective-permute-start.1
  156.1 10.6 %copy-start.9 = (bf16[256,1024]{1,0:T(8,128)(2,1)S(1)}, bf16[256,1024]{1,0:T(8,128)(2,1)}, u32[]{:S(2)}) copy-start(bf16[256,1024]{1,0:T(8,128)(2,1)} %param.7) | copy-start | bytes 1572868
  156.1 10.6 %copy-start.10 = (bf16[256,1024]{1,0:T(8,128)(2,1)S(1)}, bf16[256,1024]{1,0:T(8,128)(2,1)}, u32[]{:S(2)}) copy-start(bf16[256,1024]{1,0:T(8,128)(2,1)} %param.8) | copy-start | bytes 1572868
  166.7 10.1 %copy-start.8 = (f32[1024,128]{1,0:T(8,128)S(1)}, f32[1024,128]{1,0:T(8,128)}, u32[]{:S(2)}) copy-start(f32[1024,128]{1,0:T(8,128)} %param.9) | copy-start | bytes 1572868
  168.3 9.7 %collective-permute-start = (bf16[127,1024]{1,0:T(8,128)(2,1)S(1)}, bf16[127,1024]{1,0:T(8,128)(2,1)S(1)}, u32[]{:S(2)}, u32[]{:S(2)}) collective-permute-start(bf16[127,1024]{1,0:T(8,128)(2,1)S(1)} %slice.8), channel_id=1, source_target_pairs={{0,4},{4,8},{8,12},{12,16},{16,20},{20,24},{24,28},{28,32},{32,36}... | collective-permute-start | bytes 780296 | tf_op jit(solution)/shard_map/ppermute | solution.py:10
  178.1 10.6 %copy-start.3 = (f32[256,1024]{1,0:T(8,128)S(1)}, f32[256,1024]{1,0:T(8,128)}, u32[]{:S(2)}) copy-start(f32[256,1024]{1,0:T(8,128)} %reduce-scatter.3.cloned.1.call-done) | copy-start | bytes 3145732
  178.1 10.6 %copy-start.6 = (bf16[256,1024]{1,0:T(8,128)(2,1)S(1)}, bf16[256,1024]{1,0:T(8,128)(2,1)}, u32[]{:S(2)}) copy-start(bf16[256,1024]{1,0:T(8,128)(2,1)} %param.6) | copy-start | bytes 1572868
  188.8 1.5 copy-start.2
  190.2 225.9 %all-reduce.2.cloned.1.call-start = ((), (), s32[]{:S(2)}) async-start(), calls=%async_computation.5 | async-start | bytes 1048576 | tf_op jit(solution)/shard_map/psum | solution.py:52
  203.7 404.1 %reduce-scatter.5.cloned.1.call-start = ((), (), s32[]{:S(2)}) async-start(), calls=%async_computation.6 | async-start | bytes 17039360 | tf_op jit(solution)/shard_map/reduce_scatter | solution.py:54
  237.6 180.5 %copy-start.4 = (bf16[256,4096]{1,0:T(8,128)(2,1)S(1)}, bf16[256,4096]{1,0:T(8,128)(2,1)}, u32[]{:S(2)}) copy-start(bf16[256,4096]{1,0:T(8,128)(2,1)} %all-gather.3.cloned.1.call-done) | copy-start | bytes 6291460
Sparse Core Ops, SparseCore 0:
  10.8 85.9 all-gather.4
  104.6 44.8 reduce-scatter.2
  190.4 37.4 all-gather.2
  231.8 184.2 all-reduce.1
  421.0 186.7 reduce-scatter.4
where the time goes:
time: 615 us; the launch traced here: 614 us
  waiting for transfers between devices  522 us (85%)
  matrix products  55.7 us (9%)
  between operations  14 us (2%)
  starting transfers between devices  10.2 us (2%)
  local copies, waits for them, and re-layouts  6.47 us (1%)
    reduce_scatter x1, waiting for transfers between devices, body(): lax.psum_scatter(lax.dot_general(columns, upstream, (((0,), (0,)), ((), (...  183 us
    psum x1, waiting for transfers between devices, body(): grad_filter = lax.psum(filter_local, 'seq')  178 us
    all_gather x1, waiting for transfers between devices, body(): weight_cols = lax.all_gather(out_weight, 'seq', axis=0, tiled=True)  88.8 us
    reduce_scatter x1, waiting for transfers between devices, body(): lax.psum_scatter(partial_terms, 'ch', scatter_dimension=1, tiled=True)  45 us
    conv_general_dilated x3, matrix products, depthwise(): lax.conv_general_dilated(signal[None], kernel[:, None, :], (1,), 'VALID',...  31.8 us
    all_gather x1, waiting for transfers between devices, body(): gated_full = lax.all_gather(gated, 'ch', axis=1, tiled=True)  23.9 us
  transfers between devices with their start and end apart: 7, of which 6 were waited for; matrix products, arithmetic and copies ran while one was open for 5% of the time, Pallas kernels for 0%

commit v1 on v0

--- a/solution.py
+++ b/solution.py
@@ -49,7 +49,7 @@
     grad_key = (grad_keyed * value_stream.astype(jnp.float32)).astype(jnp.bfloat16)
     grad_value = (grad_keyed * key_stream.astype(jnp.float32)).astype(jnp.bfloat16)
     filter_local = depthwise(front_pad, grad_response)[::-1].T
-    grad_filter = lax.psum(filter_local, "seq")
+    grad_filter = jnp.sum(lax.all_gather(filter_local, "seq"), axis=0)
     columns = lax.slice_in_dim(gated_full, 0, lax.axis_size("seq") * out_weight.shape[0], axis=1)
     grad_weight = lax.psum_scatter(
         lax.dot_general(

time: 615 us -> 572 us (0.930)
  waiting for transfers between devices: 522 us -> 444 us
  local copies, waits for them, and re-layouts: 6.47 us -> 35.2 us
  other arithmetic: 5.54 us -> 12.2 us
    psum x1 -> x0, waiting for transfers between devices: 178 us -> none  [body(): grad_filter = lax.psum(filter_local, 'seq')]
    all_gather x0 -> x1, waiting for transfers between devices: none -> 128 us  [body(): grad_filter = jnp.sum(lax.all_gather(filter_local, 'seq'), axis=0)]
    unnamed x24 -> x25, local copies, waits for them, and re-layouts: 2.19 us -> 30.9 us
    reduce_scatter x1, waiting for transfers between devices: 183 us -> 156 us  [body(): lax.psum_scatter(lax.dot_general(columns, upstream, (((0,), (0,)), ((), (...]
    reduce_sum x0 -> x1, other arithmetic: none -> 6.7 us  [body(): grad_filter = jnp.sum(lax.all_gather(filter_local, 'seq'), axis=0)]
  transfers between devices with their start and end apart: 7 -> 7, of which waited for: 6 -> 6; matrix products, arithmetic and copies ran while one was open for 5% -> 12% of each run, Pallas kernels for 0% -> 0%
where the time goes in v1:
time: 572 us
  waiting for transfers between devices  444 us (78%)
  matrix products  55.7 us (10%)
  local copies, waits for them, and re-layouts  35.2 us (6%)
  between operations  14 us (2%)
  other arithmetic  12.2 us (2%)
  starting transfers between devices  10.2 us (2%)
    reduce_scatter x1, waiting for transfers between devices, body(): lax.psum_scatter(lax.dot_general(columns, upstream, (((0,), (0,)), ((), (...  156 us
    all_gather x1, waiting for transfers between devices, body(): grad_filter = jnp.sum(lax.all_gather(filter_local, 'seq'), axis=0)  128 us
    all_gather x1, waiting for transfers between devices, body(): weight_cols = lax.all_gather(out_weight, 'seq', axis=0, tiled=True)  88.8 us
    reduce_scatter x1, waiting for transfers between devices, body(): lax.psum_scatter(partial_terms, 'ch', scatter_dimension=1, tiled=True)  45 us
    conv_general_dilated x3, matrix products, depthwise(): lax.conv_general_dilated(signal[None], kernel[:, None, :], (1,), 'VALID',...  31.8 us
    unnamed x25, local copies, waits for them, and re-layouts  30.9 us
    all_gather x1, waiting for transfers between devices, body(): gated_full = lax.all_gather(gated, 'ch', axis=1, tiled=True)  23.9 us
  transfers between devices with their start and end apart: 7, of which 6 were waited for; matrix products, arithmetic and copies ran while one was open for 12% of the time, Pallas kernels for 0%

profile of v1, /device:TPU:2, one launch (start us, length us, event | category | flops | bytes accessed | tf_op | source)
XLA Modules:
  0.0 571.7 jit_solution(7199725875416674534)
XLA Ops:
  7.2 0.0 copy-start
  7.2 0.0 all-gather.7.cloned.1.call-start
  7.2 0.7 all-gather.7.cloned.1.call-update
  7.9 0.0 reduce-scatter.3.cloned.1.call-start
  8.0 88.8 %all-gather.7.cloned.1.call-done = bf16[4096,1024]{1,0:T(8,128)(2,1)} async-done(((bf16[64,1024]{1,0:T(8,128)(2,1)}), bf16[4096,1024]{1,0:T(8,128)(2,1)}) %all-gather.7.cloned.1.call-update) | async-done | bytes 8388624 | tf_op jit(solution)/shard_map/all_gather | solution.py:36
  96.8 0.0 copy-done
  96.8 7.7 %fusion.12 = f32[256,4096]{1,0:T(8,128)} fusion(bf16[256,1024]{1,0:T(8,128)(2,1)S(1)} %copy-done, bf16[4096,1024]{1,0:T(8,128)(2,1)} %all-gather.7.cloned.1.call-done), kind=kOutput, calls=%fused_computation.23 | convolution fusion | flops 2147483648 | bytes 13107200 | tf_op jit(solution)/shard_map/dot_general | solution.py:40
  104.5 0.0 reduce-scatter.3.cloned.1.call-update
  104.5 0.0 copy-start.7
  104.5 0.0 all-gather.5.cloned.1.call-start
  104.5 45.0 %reduce-scatter.3.cloned.1.call-done = f32[256,1024]{1,0:T(8,128)} async-done(((f32[256,4096]{1,0:T(8,128)}), f32[256,1024]{1,0:T(8,128)}) %reduce-scatter.3.cloned.1.call-update) | async-done | bytes 1048592 | tf_op jit(solution)/shard_map/reduce_scatter | solution.py:43
  149.5 1.4 convert_multiply_fusion.3
  150.9 0.0 copy-start.1
  151.0 1.3 collective-permute-start.1
  152.3 0.4 copy.25
  152.7 2.2 collective-permute-done.1
  154.9 1.2 maximum_bitcast_fusion
  156.1 0.0 copy-start.9
  156.1 0.0 copy-start.10
  156.1 10.6 %fusion = f32[1,256,1024]{2,0,1:T(1,128)S(1)} fusion(f32[128,1,1024]{2,1,0:T(1,128)S(1)} %copy.25, f32[1,383,1024]{2,1,0:T(8,128)S(1)} %maximum_bitcast_fusion), kind=kOutput, calls=%fused_computation.2 | convolution fusion | flops 402653184 | bytes 3141632 | tf_op jit(solution)/shard_map/conv_general_dilated | solution.py:14
  166.7 0.0 copy-start.8
  166.7 1.5 fusion.7
  168.2 0.1 slice.8
  168.3 8.5 %collective-permute-start = (bf16[127,1024]{1,0:T(8,128)(2,1)S(1)}, bf16[127,1024]{1,0:T(8,128)(2,1)S(1)}, u32[]{:S(2)}, u32[]{:S(2)}) collective-permute-start(bf16[127,1024]{1,0:T(8,128)(2,1)S(1)} %slice.8), channel_id=1, source_target_pairs={{0,4},{4,8},{8,12},{12,16},{16,20},{20,24},{24,28},{28,32},{32,36}... | collective-permute-start | bytes 780296 | tf_op jit(solution)/shard_map/ppermute | solution.py:10
  176.8 0.7 rev.6
  177.6 0.4 copy.23
  178.0 0.0 collective-permute-done
  178.0 0.1 maximum_bitcast_fusion.1
  178.1 0.0 copy-start.6
  178.2 10.6 %fusion.4 = f32[1,256,1024]{2,0,1:T(1,128)S(1)} fusion(f32[128,1,1024]{2,1,0:T(1,128)S(1)} %copy.23, bf16[1,383,1024]{2,1,0:T(8,128)(2,1)S(1)} %maximum_bitcast_fusion.1), kind=kOutput, calls=%fused_computation.12 | convolution fusion | flops 402653184 | bytes 2357248 | tf_op jit(solution)/shard_map/conv_general_dilated | solution.py:14
  188.8 1.4 fusion.10
  190.2 0.0 all-gather.5.cloned.1.call-update
  190.2 0.0 all-gather.9.cloned.1.call-start
  190.3 10.7 %fusion.2 = f32[1,128,1024]{2,0,1:T(1,128)S(1)} fusion(bf16[1,383,1024]{2,1,0:T(8,128)(2,1)S(1)} %maximum_bitcast_fusion.1, f32[256,1,1024]{2,0,1:T(8,128)S(1)} %bitcast.35), kind=kOutput, calls=%fused_computation.10 | convolution fusion | flops 402653184 | bytes 2357248 | tf_op jit(solution)/shard_map/conv_general_dilated | solution.py:14
  201.0 0.1 copy.46
  201.1 2.7 rev.7
  203.7 0.0 all-gather.9.cloned.1.call-update
  203.7 0.2 reduce-scatter.5.cloned.1.call-start
  204.0 23.9 %all-gather.5.cloned.1.call-done = bf16[256,4096]{1,0:T(8,128)(2,1)} async-done(((bf16[256,1024]{1,0:T(8,128)(2,1)}), bf16[256,4096]{1,0:T(8,128)(2,1)}) %all-gather.5.cloned.1.call-update) | async-done | bytes 2097168 | tf_op jit(solution)/shard_map/all_gather | solution.py:35
  227.9 9.7 %fusion.13 = f32[4096,1024]{1,0:T(8,128)} fusion(bf16[256,4096]{1,0:T(8,128)(2,1)} %all-gather.5.cloned.1.call-done, bf16[256,1024]{1,0:T(8,128)(2,1)S(1)} %copy-done), kind=kOutput, calls=%fused_computation.24 | convolution fusion | flops 2147483648 | bytes 19398656 | tf_op jit(solution)/shard_map/dot_general | solution.py:55
  237.6 0.0 reduce-scatter.5.cloned.1.call-update
  237.6 1.6 copy-done.4
  239.2 6.5 %convolution_convert_fusion = bf16[256,1024]{1,0:T(8,128)(2,1)} fusion(bf16[256,4096]{1,0:T(8,128)(2,1)S(1)} %copy-done.4, bf16[4096,1024]{1,0:T(8,128)(2,1)} %all-gather.7.cloned.1.call-done), kind=kOutput, calls=%fused_computation.9 | convolution fusion | flops 2147745792 | bytes 11010048 | tf_op jit(solution)/shard_map/dot_general | solution.py:37
  245.7 127.8 %all-gather.9.cloned.1.call-done = f32[65536,128]{0,1:T(8,128)} async-done(((f32[1024,128]{0,1:T(8,128)}), f32[65536,128]{0,1:T(8,128)}) %all-gather.9.cloned.1.call-update) | async-done | bytes 33554448 | tf_op jit(solution)/shard_map/all_gather | solution.py:52
  373.4 28.2 %copy.32 = f32[16,8,64,1024]{3,2,1,0:T(8,128)S(1)} copy(f32[16,8,64,1024]{3,1,2,0:T(8,128)} %bitcast.34) | data formatting | bytes 67108864
  401.6 6.7 %bitcast_reduce_fusion = f32[1024,128]{0,1:T(8,128)S(1)} fusion(f32[16,8,64,1024]{3,2,1,0:T(8,128)S(1)} %copy.32), kind=kLoop, calls=%fused_computation | loop fusion | flops 8257536 | bytes 34078720 | tf_op jit(solution)/shard_map/reduce_sum | solution.py:52
  408.4 1.0 copy.28
  409.4 155.8 %reduce-scatter.5.cloned.1.call-done = f32[64,1024]{1,0:T(8,128)} async-done(((f32[4096,1024]{1,0:T(8,128)}), f32[64,1024]{1,0:T(8,128)}) %reduce-scatter.5.cloned.1.call-update) | async-done | bytes 262160 | tf_op jit(solution)/shard_map/reduce_scatter | solution.py:54
  (14 shorter events, 0.1 us)
Async XLA Ops:
  7.2 89.6 %copy-start = (bf16[256,1024]{1,0:T(8,128)(2,1)S(1)}, bf16[256,1024]{1,0:T(8,128)(2,1)}, u32[]{:S(2)}) copy-start(bf16[256,1024]{1,0:T(8,128)(2,1)} %param.11) | copy-start | bytes 1572868
  7.2 89.6 %all-gather.7.cloned.1.call-start = ((), (), s32[]{:S(2)}) async-start(), calls=%async_computation.3 | async-start | bytes 8519680 | tf_op jit(solution)/shard_map/all_gather | solution.py:36
  7.9 141.6 %reduce-scatter.3.cloned.1.call-start = ((), (), s32[]{:S(2)}) async-start(), calls=%async_computation.4 | async-start | bytes 5242880 | tf_op jit(solution)/shard_map/reduce_scatter | solution.py:43
  104.4 45.1 %copy-start.5 = (bf16[256,1024]{1,0:T(8,128)(2,1)S(1)}, bf16[256,1024]{1,0:T(8,128)(2,1)}, u32[]{:S(2)}) copy-start(bf16[256,1024]{1,0:T(8,128)(2,1)} %param.6) | copy-start | bytes 1572868
  104.5 47.8 %copy-start.7 = (f32[1024,128]{1,0:T(8,128)S(1)}, f32[1024,128]{1,0:T(8,128)}, u32[]{:S(2)}) copy-start(f32[1024,128]{1,0:T(8,128)} %param.9) | copy-start | bytes 1572868
  104.5 123.4 %all-gather.5.cloned.1.call-start = ((), (), s32[]{:S(2)}) async-start(), calls=%async_computation.2 | async-start | bytes 2621440 | tf_op jit(solution)/shard_map/all_gather | solution.py:35
  150.9 5.2 copy-start.1
  151.0 3.9 collective-permute-start.1
  156.1 10.6 %copy-start.9 = (bf16[256,1024]{1,0:T(8,128)(2,1)S(1)}, bf16[256,1024]{1,0:T(8,128)(2,1)}, u32[]{:S(2)}) copy-start(bf16[256,1024]{1,0:T(8,128)(2,1)} %param.7) | copy-start | bytes 1572868
  156.1 10.6 %copy-start.10 = (bf16[256,1024]{1,0:T(8,128)(2,1)S(1)}, bf16[256,1024]{1,0:T(8,128)(2,1)}, u32[]{:S(2)}) copy-start(bf16[256,1024]{1,0:T(8,128)(2,1)} %param.8) | copy-start | bytes 1572868
  166.7 10.1 %copy-start.8 = (f32[1024,128]{1,0:T(8,128)S(1)}, f32[1024,128]{1,0:T(8,128)}, u32[]{:S(2)}) copy-start(f32[1024,128]{1,0:T(8,128)} %param.9) | copy-start | bytes 1572868
  168.3 9.7 %collective-permute-start = (bf16[127,1024]{1,0:T(8,128)(2,1)S(1)}, bf16[127,1024]{1,0:T(8,128)(2,1)S(1)}, u32[]{:S(2)}, u32[]{:S(2)}) collective-permute-start(bf16[127,1024]{1,0:T(8,128)(2,1)S(1)} %slice.8), channel_id=1, source_target_pairs={{0,4},{4,8},{8,12},{12,16},{16,20},{20,24},{24,28},{28,32},{32,36}... | collective-permute-start | bytes 780296 | tf_op jit(solution)/shard_map/ppermute | solution.py:10
  178.1 10.6 %copy-start.3 = (f32[256,1024]{1,0:T(8,128)S(1)}, f32[256,1024]{1,0:T(8,128)}, u32[]{:S(2)}) copy-start(f32[256,1024]{1,0:T(8,128)} %reduce-scatter.3.cloned.1.call-done) | copy-start | bytes 3145732
  178.1 10.6 %copy-start.6 = (bf16[256,1024]{1,0:T(8,128)(2,1)S(1)}, bf16[256,1024]{1,0:T(8,128)(2,1)}, u32[]{:S(2)}) copy-start(bf16[256,1024]{1,0:T(8,128)(2,1)} %param.6) | copy-start | bytes 1572868
  188.8 1.5 copy-start.2
  190.2 183.2 %all-gather.9.cloned.1.call-start = ((), (), s32[]{:S(2)}) async-start(), calls=%async_computation.6 | async-start | bytes 34078720 | tf_op jit(solution)/shard_map/all_gather | solution.py:52
  203.7 361.4 %reduce-scatter.5.cloned.1.call-start = ((), (), s32[]{:S(2)}) async-start(), calls=%async_computation.5 | async-start | bytes 17039360 | tf_op jit(solution)/shard_map/reduce_scatter | solution.py:54
  237.6 1.6 copy-start.4
Sparse Core Ops, SparseCore 0:
  10.8 85.9 all-gather.6
  104.6 44.8 reduce-scatter.2
  190.4 37.4 all-gather.4
  230.5 142.8 all-gather.8
  378.3 186.7 reduce-scatter.4
